TPU v7x, 32 devices: a whole 2x2x4 slice. The times are simulated.
32 devices in a mesh: ctx: 4 (over y, core), row: 8 (over z, x).
Axes of the slice: x: 2, y: 2, z: 4, core: 2. Of those that a mesh axis runs over, the one named last changes fastest.
Arguments:
- queries: bfloat16 [16, 2, 4096], P('row'), may hold values from -400 to 400
- prefix_id: int32 [16], P('row'), may hold values from 0 to 7
- prefix_keys: bfloat16 [8, 1024, 512], P(None, ('ctx', 'row')), may hold values from -8 to 8
- prefix_values: bfloat16 [8, 1024, 512], P(None, ('ctx', 'row')), may hold values from -6 to 6
- pool_keys: bfloat16 [512, 64, 512], P(('ctx', 'row')), may hold values from -5 to 5
- pool_values: bfloat16 [512, 64, 512], P(('ctx', 'row')), may hold values from -6 to 6
- page_table: int32 [16, 32], P('row'), may hold values from 0 to 511, as said below
- suffix_len: int32 [16], P('row'), may hold values from 256 to 2048
- new_keys: bfloat16 [16, 2, 512], P('row'), may hold values from -6.25 to 6.25
- new_values: bfloat16 [16, 2, 512], P('row'), may hold values from -6 to 6
Outputs:
- attended: bfloat16 [16, 2, 4096], P('row')
Inputs may be any that keep to these rules, and one draw needn't show every extreme that they name: `page_table`: the 64 entries of the rows i with one value of i // 2 name different pool pages p with (p // 16) % (8) == i // 2, and together they name all such pages.
All inputs are finite; a program needn't handle non-finite values.
Results may differ from a plain program's by a relative error of at most 0.003.
Values may be sent and summed in bfloat16 or wider, within the bound.
No kernel may reach another device: no remote copies, remote signals or barrier semaphores. Data moves between devices by JAX's collectives and lax.ppermute only.
A program may use at most 64 MiB of HBM per device.

v0:
```python
import math
import jax
import jax.numpy as jnp
from jax import lax
from jax.sharding import PartitionSpec as P

H = 32
KVH = 4
HD = 128
LANES = 128
MASKED_SCORE = -1e30


def block_stats(scores, valid_mask, values, einsum_form):
    block_peak = jnp.max(jnp.where(valid_mask, scores, MASKED_SCORE), axis=-1)
    weights = jnp.where(valid_mask, jnp.exp(scores - block_peak[..., None]), 0.0).astype(
        jnp.bfloat16
    )
    block_total = jnp.sum(weights.astype(jnp.float32), axis=-1)
    block_sum = jnp.einsum(einsum_form, weights, values, preferred_element_type=jnp.float32)
    return (block_peak, block_total, block_sum)


def combine_pair(earlier, later):
    highest = jnp.maximum(earlier[0], later[0])
    left_factor = jnp.exp(earlier[0] - highest)
    right_factor = jnp.exp(later[0] - highest)
    totals = left_factor * earlier[1] + right_factor * later[1]
    sums = left_factor[..., None] * earlier[2] + right_factor[..., None] * later[2]
    return (highest, totals, sums)


def per_device(
    queries,
    prefix_id,
    prefix_keys,
    prefix_values,
    pool_keys,
    pool_values,
    page_table,
    suffix_len,
    new_keys,
    new_values,
):
    rows_dev, step_count, feature_width = queries.shape
    groups = H // KVH
    score_scale = 1.0 / math.sqrt(HD)
    row_count = lax.axis_size("row")
    ctx_count = lax.axis_size("ctx")
    row_index = lax.axis_index("row")
    ctx_index = lax.axis_index("ctx")
    flat_index = ctx_index * row_count + row_index
    own_query = queries.reshape(rows_dev, step_count, KVH, groups, HD)
    slot_count, page_len, kv_width = pool_keys.shape
    slot_ids = flat_index * slot_count + jnp.arange(slot_count, dtype=jnp.int32)
    slot_match = page_table[:, :, None] == slot_ids[None, None, :]
    entry_pos = jnp.arange(page_table.shape[1], dtype=jnp.int32)
    page_of = jnp.sum(jnp.where(slot_match, entry_pos[None, :, None], 0), axis=1)
    owned = jnp.any(slot_match, axis=1)
    token_pos = (
        page_of[:, :, None] * page_len + jnp.arange(page_len, dtype=jnp.int32)[None, None, :]
    )
    live_mask = owned[:, :, None] & (token_pos < suffix_len[:, None, None])
    live_mask = live_mask.reshape(rows_dev, 1, 1, 1, slot_count * page_len)
    flat_keys = pool_keys.reshape(slot_count * page_len, KVH, HD)
    flat_values = pool_values.reshape(slot_count * page_len, KVH, HD)
    suffix_scores = (
        jnp.einsum("rskgd,tkd->rskgt", own_query, flat_keys, preferred_element_type=jnp.float32)
        * score_scale
    )
    suffix_stats = block_stats(suffix_scores, live_mask, flat_values, "rskgt,tkd->rskgd")
    fresh_keys = new_keys.reshape(rows_dev, step_count, KVH, HD)
    fresh_values = new_values.reshape(rows_dev, step_count, KVH, HD)
    fresh_scores = (
        jnp.einsum("rskgd,rtkd->rskgt", own_query, fresh_keys, preferred_element_type=jnp.float32)
        * score_scale
    )
    causal = jnp.arange(step_count)[None, :] <= jnp.arange(step_count)[:, None]
    causal = causal.reshape(1, step_count, 1, 1, step_count)
    fresh_stats = block_stats(fresh_scores, causal, fresh_values, "rskgt,rtkd->rskgd")
    query_cols = step_count * feature_width
    id_cols = jnp.broadcast_to(prefix_id.astype(jnp.bfloat16)[:, None], (rows_dev, LANES))
    packed = jnp.concatenate([queries.reshape(rows_dev, query_cols), id_cols], axis=1)
    gathered = lax.all_gather(packed, "row", axis=0, tiled=True)
    total_rows = gathered.shape[0]
    every_query = gathered[:, :query_cols].reshape(total_rows, step_count, KVH, groups, HD)
    every_prefix = gathered[:, query_cols].astype(jnp.int32)
    span_len = prefix_keys.shape[1]
    row_keys = jnp.take(prefix_keys, every_prefix, axis=0).reshape(total_rows, span_len, KVH, HD)
    row_values = jnp.take(prefix_values, every_prefix, axis=0).reshape(
        total_rows, span_len, KVH, HD
    )
    prefix_scores = (
        jnp.einsum("rskgd,rtkd->rskgt", every_query, row_keys, preferred_element_type=jnp.float32)
        * score_scale
    )
    always = jnp.ones((1, 1, 1, 1, span_len), dtype=bool)
    prefix_stats = block_stats(prefix_scores, always, row_values, "rskgt,rtkd->rskgd")
    row_start = row_index * rows_dev
    own_prefix = tuple(
        (lax.dynamic_slice_in_dim(member, row_start, rows_dev, 0) for member in prefix_stats)
    )
    own_merged = combine_pair(own_prefix, suffix_stats)
    peak_all, total_all, sum_all = tuple(
        (
            lax.dynamic_update_slice_in_dim(whole_arr, piece_arr, row_start, 0)
            for whole_arr, piece_arr in zip(prefix_stats, own_merged)
        )
    )
    units = rows_dev * step_count * H
    share = units // ctx_count
    pt_rows = -(-2 * share // LANES)
    peak_u = peak_all.reshape(row_count, ctx_count, share)
    total_u = total_all.reshape(row_count, ctx_count, share)
    sum_u = sum_all.reshape(row_count, ctx_count, share, HD)
    pt = jnp.concatenate([peak_u, total_u], axis=-1)
    pt = jnp.pad(pt, ((0, 0), (0, 0), (0, pt_rows * LANES - 2 * share)))
    pt = pt.reshape(row_count, ctx_count, pt_rows, LANES)
    outgoing = jnp.concatenate([sum_u, pt], axis=2)
    outgoing = jnp.swapaxes(outgoing, 0, 1).reshape(ctx_count * row_count, share + pt_rows, LANES)
    incoming = lax.all_to_all(outgoing, ("ctx", "row"), split_axis=0, concat_axis=0, tiled=True)
    sources = incoming.shape[0]
    got_sum = incoming[:, :share, :]
    got_pt = incoming[:, share:, :].reshape(sources, pt_rows * LANES)
    got_peak = got_pt[:, :share]
    got_total = got_pt[:, share : 2 * share]
    unit_start = ctx_index * share
    fresh_peak = lax.dynamic_slice_in_dim(fresh_stats[0].reshape(units), unit_start, share)
    fresh_total = lax.dynamic_slice_in_dim(fresh_stats[1].reshape(units), unit_start, share)
    fresh_sum = lax.dynamic_slice_in_dim(fresh_stats[2].reshape(units, HD), unit_start, share)
    top = jnp.maximum(jnp.max(got_peak, axis=0), fresh_peak)
    factor = jnp.exp(got_peak - top[None])
    fresh_factor = jnp.exp(fresh_peak - top)
    denom = jnp.sum(factor * got_total, axis=0) + fresh_factor * fresh_total
    numer = jnp.sum(factor[..., None] * got_sum, axis=0) + fresh_factor[..., None] * fresh_sum
    result = (numer / denom[..., None]).astype(jnp.bfloat16)
    whole = lax.all_gather(result, "ctx", axis=0, tiled=True)
    return whole.reshape(rows_dev, step_count, H * HD)


def solution(mesh):
    in_specs = (
        P("row", None, None),
        P("row"),
        P(None, ("ctx", "row"), None),
        P(None, ("ctx", "row"), None),
        P(("ctx", "row"), None, None),
        P(("ctx", "row"), None, None),
        P("row", None),
        P("row"),
        P("row", None, None),
        P("row", None, None),
    )
    out_specs = P("row", None, None)
    return jax.shard_map(
        per_device, mesh=mesh, in_specs=in_specs, out_specs=out_specs, check_vma=False
    )
```

profile of v0, /device:TPU:0, one launch (start us, length us, event | category | flops | bytes accessed | tf_op | source)
XLA Modules:
  0.0 77.9 jit_solution(5196668622109800049)
XLA Ops:
  0.0 0.7 convert_element_type.32
  0.7 0.8 %copy.117 = bf16[1,2,2,4096]{3,1,2,0:T(2,128)(2,1)S(1)} copy(bf16[1,2,2,4096]{3,2,1,0:T(2,128)(2,1)} %bitcast.69) | data formatting | bytes 65536
  1.6 32.5 %all-gather = bf16[8,2,8320]{2,1,0:T(2,128)(2,1)S(1)} all-gather(bf16[1,2,8320]{2,1,0:T(2,128)(2,1)S(1)} %maximum_bitcast_fusion.1), channel_id=1, replica_groups=mesh['ctx'=4,'row'=8] {'row'}, dimensions={0}, use_global_device_ids=true | all-gather | bytes 299520 | tf_op jit(solution)/shard_map/all_gather | solution.py:84
  34.5 0.7 copy-done.10
  35.1 0.2 compare_reduce_fusion
  35.3 0.2 fusion.16
  35.6 0.6 gather_fusion
  36.2 0.4 copy-done.3
  36.5 0.6 gather_fusion.1
  37.1 0.2 broadcast_select_fusion.1
  37.3 0.1 reshape.127
  37.6 0.5 fusion.22
  38.1 0.5 convert_reduce_fusion.1
  38.6 0.3 fusion.10
  39.3 0.5 copy-done.1
  39.8 0.3 reshape.130
  40.1 0.6 copy-done.11
  40.8 0.5 select_reduce_fusion
  41.4 0.9 %convert_reduce_fusion = (f32[2,2,4,8]{3,1,0,2:T(2,128)S(1)}, bf16[2,2,4,8,1024]{4,3,1,0,2:T(8,128)(2,1)}) fusion(f32[2,2,4,8,1024]{4,3,1,0,2:T(8,128)S(1)} %get-tuple-element.23, f32[2,2,4,8]{3,1,0,2:T(2,128)S(1)} %get-tuple-element.22, pred[2,1024]{1,0:T(4,128)(4,1)S(1)} %compare_and_fusion), kind=kLoop, calls=%fused_computation.22 | loop fusion | flops 655232 | bytes 789504 | tf_op jit(solution)/shard_map/reduce_sum | solution.py:19
  42.2 0.6 fusion.19
  43.2 0.3 reshape.132
  43.5 0.4 copy-done.7
  43.9 1.2 %fusion.4 = f32[16,2,4,8,128]{4,3,1,2,0:T(8,128)S(1)} fusion(f32[16,2,4,8,128]{4,3,1,2,0:T(8,128)S(1)} %copy.164, s32[]{:T(128)S(6)} %select_n.41, bf16[1024,4,128,1,1]{2,1,0,4,3:T(4,128)(2,1)S(1)} %bitcast.63, bf16[2,2,4,8,1024]{4,3,1,0,2:T(8,128)(2,1)} %get-tuple-element.16, f32[16,4,128,2,8]{2,4,3,1,0:T(8,128)S(1)} %fusion.10, ...), kind=kOutput, calls=%fused_computation.10 | convolution fusion | flops 33603584 | bytes 1458180 | tf_op jit(solution)/shard_map/rskgt,tkd->rskgd/dot_general | solution.py:20
  45.3 0.3 copy.161
  45.7 1.2 %copy.96 = f32[32,33,128]{2,1,0:T(8,128)} copy(f32[32,33,128]{2,0,1:T(8,128)S(1)} %bitcast.59) | data formatting | bytes 1081344 | tf_op jit(solution)/shard_map/reshape | solution.py:120
  46.8 5.5 %all-to-all-start = ((f32[32,33,128]{2,1,0:T(8,128)}), f32[32,33,128]{2,1,0:T(8,128)S(1)}, u32[]{:S(2)}, u32[]{:S(2)}) async-start(f32[32,33,128]{2,1,0:T(8,128)} %copy.96), calls=%async_computation | async-start | bytes 1310720 | tf_op jit(solution)/shard_map/all_to_all | solution.py:121
  52.4 0.3 select_reduce_fusion.1
  52.9 0.2 convolution_bitcast_fusion
  53.2 18.3 %all-to-all-done = f32[32,33,128]{2,1,0:T(8,128)S(1)} async-done(((f32[32,33,128]{2,1,0:T(8,128)}), f32[32,33,128]{2,1,0:T(8,128)S(1)}, u32[]{:S(2)}, u32[]{:S(2)}) %all-to-all-start) | async-done | bytes 540704 | tf_op jit(solution)/shard_map/all_to_all | solution.py:121
  71.8 0.2 fusion.8
  72.1 5.2 %all_gather.7 = bf16[128,128]{1,0:T(8,128)(2,1)S(1)} all-gather(bf16[32,128]{1,0:T(8,128)(2,1)S(1)} %divide_convert_fusion), channel_id=1, replica_groups=mesh['ctx'=4,'row'=8] {'ctx'}, dimensions={0}, use_global_device_ids=true | all-gather | bytes 40960 | tf_op jit(solution)/shard_map/all_gather | solution.py:137
  77.3 0.6 reshape.144
  (62 shorter events, 2.3 us)
Async XLA Ops:
  0.0 35.6 %copy-start = (bf16[8,32,512]{2,1,0:T(8,128)(2,1)S(1)}, bf16[8,32,512]{2,1,0:T(8,128)(2,1)}, u32[]{:S(2)}) copy-start(bf16[8,32,512]{2,1,0:T(8,128)(2,1)} %param.15) | copy-start | bytes 786436
  34.4 1.1 %copy-start.4 = (bf16[2,2,4096]{2,1,0:T(2,128)(2,1)S(1)}, bf16[2,2,4096]{2,1,0:T(2,128)(2,1)}, u32[]{:S(2)}) copy-start(bf16[2,2,4096]{2,1,0:T(2,128)(2,1)} %param.12) | copy-start | bytes 98308
  34.4 0.7 copy-start.10
  35.5 5.3 %copy-start.5 = (bf16[2,2,4,8,128]{4,3,2,1,0:T(8,128)(2,1)}, bf16[2,2,4,8,128]{4,3,2,1,0:T(8,128)(2,1)S(1)}, u32[]{:S(2)}) copy-start(bf16[2,2,4,8,128]{4,3,2,1,0:T(8,128)(2,1)S(1)} %reshape.131) | copy-start | bytes 98308
  35.6 1.0 %copy-start.3 = (bf16[8,32,512]{2,1,0:T(8,128)(2,1)S(1)}, bf16[8,32,512]{2,1,0:T(8,128)(2,1)}, u32[]{:S(2)}) copy-start(bf16[8,32,512]{2,1,0:T(8,128)(2,1)} %param.14) | copy-start | bytes 786436
  38.6 1.2 %copy-start.1 = (bf16[16,64,512]{2,1,0:T(8,128)(2,1)S(1)}, bf16[16,64,512]{2,1,0:T(8,128)(2,1)}, u32[]{:S(2)}) copy-start(bf16[16,64,512]{2,1,0:T(8,128)(2,1)} %param.16) | copy-start | bytes 3145732
  40.1 0.7 copy-start.11
  41.4 1.8 %copy-start.2 = (bf16[16,64,512]{2,1,0:T(8,128)(2,1)S(1)}, bf16[16,64,512]{2,1,0:T(8,128)(2,1)}, u32[]{:S(2)}) copy-start(bf16[16,64,512]{2,1,0:T(8,128)(2,1)} %param.17) | copy-start | bytes 3145732
  43.2 0.7 copy-start.7
  43.2 0.7 copy-start.8
  46.8 5.6 %copy-start.6 = (bf16[2,2,4,8,128]{4,3,2,1,0:T(8,128)(2,1)S(1)}, bf16[2,2,4,8,128]{4,3,2,1,0:T(8,128)(2,1)}, u32[]{:S(2)}) copy-start(bf16[2,2,4,8,128]{4,3,2,1,0:T(8,128)(2,1)} %copy-done.5) | copy-start | bytes 98308
  46.8 5.6 %copy-start.12 = (bf16[2,2,512]{2,1,0:T(2,128)(2,1)S(1)}, bf16[2,2,512]{2,1,0:T(2,128)(2,1)}, u32[]{:S(2)}) copy-start(bf16[2,2,512]{2,1,0:T(2,128)(2,1)} %param.20) | copy-start | bytes 12292
  46.8 6.1 %copy-start.9 = (bf16[2,2,512]{2,1,0:T(2,128)(2,1)S(1)}, bf16[2,2,512]{2,1,0:T(2,128)(2,1)}, u32[]{:S(2)}) copy-start(bf16[2,2,512]{2,1,0:T(2,128)(2,1)} %param.21) | copy-start | bytes 12292
  46.8 24.7 %all-to-all-start = ((f32[32,33,128]{2,1,0:T(8,128)}), f32[32,33,128]{2,1,0:T(8,128)S(1)}, u32[]{:S(2)}, u32[]{:S(2)}) async-start(f32[32,33,128]{2,1,0:T(8,128)} %copy.96), calls=%async_computation | async-start | bytes 1310720 | tf_op jit(solution)/shard_map/all_to_all | solution.py:121
where the time goes:
time: 78.4 us; the launch traced here: 77.9 us
  blocking collectives  37.7 us (48%)
  waiting for transfers between devices  18.3 us (23%)
  local copies, waits for them, and re-layouts  8.64 us (11%)
  starting transfers between devices  5.54 us (7%)
  other arithmetic  4.24 us (5%)
  matrix products  3.09 us (4%)
    all_gather x1, blocking collectives, per_device(): gathered = lax.all_gather(packed, 'row', axis=0, tiled=True)  32.5 us
    all_to_all x1, waiting for transfers between devices, per_device(): lax.all_to_all(outgoing, ('ctx', 'row'), split_axis=0, concat_axis=0, til...  18.3 us
    all_to_all x1, starting transfers between devices, per_device(): lax.all_to_all(outgoing, ('ctx', 'row'), split_axis=0, concat_axis=0, til...  5.54 us
    all_gather x1, blocking collectives, per_device(): whole = lax.all_gather(result, 'ctx', axis=0, tiled=True)  5.18 us
    unnamed x31, local copies, waits for them, and re-layouts  3.59 us
    dot_general x3, matrix products, block_stats(): jnp.einsum(einsum_form, weights, values, preferred_element_type=jnp.float32)  1.75 us
  transfers between devices with their start and end apart: 1, of which 1 were waited for; matrix products, arithmetic and copies ran while one was open for 1% of the time, Pallas kernels for 0%

commit v1 on v0

--- a/solution.py
+++ b/solution.py
@@ -81,7 +81,16 @@
     query_cols = step_count * feature_width
     id_cols = jnp.broadcast_to(prefix_id.astype(jnp.bfloat16)[:, None], (rows_dev, LANES))
     packed = jnp.concatenate([queries.reshape(rows_dev, query_cols), id_cols], axis=1)
-    gathered = lax.all_gather(packed, "row", axis=0, tiled=True)
+    ways = lax.axis_size("row")
+    up = [(d, (d + 1) % ways) for d in range(ways)]
+    down = [(d, (d - 1) % ways) for d in range(ways)]
+    earlier_2, later_2 = ([packed], [packed])
+    for _ in range(ways // 2):
+        earlier_2.append(lax.ppermute(earlier_2[-1], "row", up))
+    for _ in range((ways - 1) // 2):
+        later_2.append(lax.ppermute(later_2[-1], "row", down))
+    line = jnp.concatenate([*earlier_2[::-1], *later_2[1:]], axis=0)
+    gathered = jnp.roll(line, (lax.axis_index("row") - ways // 2) * packed.shape[0], axis=0)
     total_rows = gathered.shape[0]
     every_query = gathered[:, :query_cols].reshape(total_rows, step_count, KVH, groups, HD)
     every_prefix = gathered[:, query_cols].astype(jnp.int32)

time: 78.4 us -> 68.2 us (0.87)
  blocking collectives: 37.7 us -> 5.18 us
  starting transfers between devices: 5.54 us -> 18.4 us
  waiting for transfers between devices: 18.3 us -> 25.3 us
  local copies, waits for them, and re-layouts: 8.64 us -> 13.3 us
  other arithmetic: 4.24 us -> 3.13 us
  matrix products: 3.09 us -> 2.14 us
    all_gather x1 -> x0, blocking collectives: 32.5 us -> none  [per_device(): gathered = lax.all_gather(packed, 'row', axis=0, tiled=True)]
    ppermute x0 -> x7, starting transfers between devices: none -> 15.7 us  [the longest x3 12.7 us: per_device(): later_2.append(lax.ppermute(later_2[-1], 'row', down))]
    ppermute x0 -> x7, waiting for transfers between devices: none -> 6.98 us  [the longest x4 6.27 us: per_device(): earlier_2.append(lax.ppermute(earlier_2[-1], 'row', up))]
    concatenate x0 -> x1, local copies, waits for them, and re-layouts: none -> 3.19 us  [per_device(): jnp.roll(line, (lax.axis_index('row') - ways // 2) * packed.shape[0], axi...]
    all_to_all x1, starting transfers between devices: 5.54 us -> 2.75 us  [per_device(): lax.all_to_all(outgoing, ('ctx', 'row'), split_axis=0, concat_axis=0, til...]
    reshape x1, local copies, waits for them, and re-layouts: 0.27 us -> 1.35 us  [per_device(): flat_keys = pool_keys.reshape(slot_count * page_len, KVH, HD)]
    dot_general x3, matrix products: 1.75 us -> 0.81 us  [block_stats(): jnp.einsum(einsum_form, weights, values, preferred_element_type=jnp.float32)]
    reshape x1, local copies, waits for them, and re-layouts: 0.29 us -> 1.13 us  [per_device(): flat_values = pool_values.reshape(slot_count * page_len, KVH, HD)]
  transfers between devices with their start and end apart: 1 -> 8, of which waited for: 1 -> 6; matrix products, arithmetic and copies ran while one was open for 1% -> 7% of each run, Pallas kernels for 0% -> 0%
where the time goes in v1:
time: 68.2 us; the launch traced here: 67.8 us
  waiting for transfers between devices  25.3 us (37%)
  starting transfers between devices  18.4 us (27%)
  local copies, waits for them, and re-layouts  13.3 us (20%)
  blocking collectives  5.18 us (8%)
  other arithmetic  3.13 us (5%)
  matrix products  2.14 us (3%)
    all_to_all x1, waiting for transfers between devices, per_device(): lax.all_to_all(outgoing, ('ctx', 'row'), split_axis=0, concat_axis=0, til...  18.3 us
    ppermute x3, starting transfers between devices, per_device(): later_2.append(lax.ppermute(later_2[-1], 'row', down))  12.7 us
    ppermute x4, waiting for transfers between devices, per_device(): earlier_2.append(lax.ppermute(earlier_2[-1], 'row', up))  6.27 us
    all_gather x1, blocking collectives, per_device(): whole = lax.all_gather(result, 'ctx', axis=0, tiled=True)  5.18 us
    concatenate x1, local copies, waits for them, and re-layouts, per_device(): jnp.roll(line, (lax.axis_index('row') - ways // 2) * packed.shape[0], axi...  3.19 us
    unnamed x22, local copies, waits for them, and re-layouts  3.11 us
    ppermute x4, starting transfers between devices, per_device(): earlier_2.append(lax.ppermute(earlier_2[-1], 'row', up))  3 us
    all_to_all x1, starting transfers between devices, per_device(): lax.all_to_all(outgoing, ('ctx', 'row'), split_axis=0, concat_axis=0, til...  2.75 us
  transfers between devices with their start and end apart: 8, of which 6 were waited for; matrix products, arithmetic and copies ran while one was open for 7% of the time, Pallas kernels for 0%

profile of v1, /device:TPU:0, one launch (start us, length us, event | category | flops | bytes accessed | tf_op | source)
XLA Modules:
  0.0 67.8 jit_solution(7213206947805654114)
XLA Ops:
  0.0 0.7 %convert_element_type.32 = bf16[2]{0:T(256)(128)(2,1)S(1)} convert(s32[2]{0:T(128)} %param.13) | non-fusion elementwise | flops 2 | bytes 12 | tf_op jit(solution)/shard_map/convert_element_type | solution.py:82
  0.7 0.8 %copy.117 = bf16[1,2,2,4096]{3,1,2,0:T(2,128)(2,1)S(1)} copy(bf16[1,2,2,4096]{3,2,1,0:T(2,128)(2,1)} %bitcast.67) | data formatting | bytes 65536
  1.6 3.0 %collective-permute-start = (bf16[2,8320]{1,0:T(2,128)(2,1)S(1)}, bf16[2,8320]{1,0:T(2,128)(2,1)S(1)}, u32[]{:S(2)}, u32[]{:S(2)}) collective-permute-start(bf16[2,8320]{1,0:T(2,128)(2,1)S(1)} %pad_maximum_fusion), channel_id=1, source_target_pairs={{0,1},{1,2},{2,3},{3,4},{4,5},{5,6},{6,7},{7,0},{8,9},{9,10},{10,1... | collective-permute-start | bytes 99848 | tf_op jit(solution)/shard_map/ppermute | solution.py:89
  4.6 3.1 %collective-permute-start.4 = (bf16[2,8320]{1,0:T(2,128)(2,1)S(1)}, bf16[2,8320]{1,0:T(2,128)(2,1)S(1)}, u32[]{:S(2)}, u32[]{:S(2)}) collective-permute-start(bf16[2,8320]{1,0:T(2,128)(2,1)S(1)} %pad_maximum_fusion), channel_id=1, source_target_pairs={{0,7},{1,0},{2,1},{3,2},{4,3},{5,4},{6,5},{7,6},{8,15},{9,8},{10,9... | collective-permute-start | bytes 99848 | tf_op jit(solution)/shard_map/ppermute | solution.py:91
  7.7 0.7 copy-done.6
  9.2 0.4 collective-permute-done
  9.9 1.3 %reshape.130 = bf16[1024,4,128]{2,1,0:T(4,128)(2,1)S(1)} reshape(bf16[16,64,512]{2,1,0:T(8,128)(2,1)} %param.16) | data formatting | bytes 2097152 | tf_op jit(solution)/shard_map/reshape | solution.py:65
  11.2 4.6 %collective-permute-start.5 = (bf16[2,8320]{1,0:T(2,128)(2,1)S(1)}, bf16[2,8320]{1,0:T(2,128)(2,1)S(1)}, u32[]{:S(2)}, u32[]{:S(2)}) collective-permute-start(bf16[2,8320]{1,0:T(2,128)(2,1)S(1)} %collective-permute-done.4), channel_id=1, source_target_pairs={{0,7},{1,0},{2,1},{3,2},{4,3},{5,4},{6,5},{7,6},{8,15},{9,8},{10,9... | collective-permute-start | bytes 99848 | tf_op jit(solution)/shard_map/ppermute | solution.py:91
  15.8 0.4 collective-permute-done.1
  16.2 0.5 select_reduce_fusion
  16.7 0.7 %collective-permute-done.5 = bf16[2,8320]{1,0:T(2,128)(2,1)S(1)} collective-permute-done((bf16[2,8320]{1,0:T(2,128)(2,1)S(1)}, bf16[2,8320]{1,0:T(2,128)(2,1)S(1)}, u32[]{:S(2)}, u32[]{:S(2)}) %collective-permute-start.5) | collective-permute-done | bytes 33312 | tf_op jit(solution)/shard_map/ppermute | solution.py:91
  17.4 5.0 %collective-permute-start.6 = (bf16[2,8320]{1,0:T(2,128)(2,1)S(1)}, bf16[2,8320]{1,0:T(2,128)(2,1)S(1)}, u32[]{:S(2)}, u32[]{:S(2)}) collective-permute-start(bf16[2,8320]{1,0:T(2,128)(2,1)S(1)} %collective-permute-done.5), channel_id=1, source_target_pairs={{0,7},{1,0},{2,1},{3,2},{4,3},{5,4},{6,5},{7,6},{8,15},{9,8},{10,9... | collective-permute-start | bytes 99848 | tf_op jit(solution)/shard_map/ppermute | solution.py:91
  22.4 0.4 collective-permute-done.2
  22.8 0.3 convert_reduce_fusion
  23.1 1.1 %reshape.132 = bf16[1024,4,128]{2,1,0:T(4,128)(2,1)} reshape(bf16[16,64,512]{2,1,0:T(8,128)(2,1)S(1)} %copy-done.1) | data formatting | bytes 2097152 | tf_op jit(solution)/shard_map/reshape | solution.py:66
  24.2 5.2 %collective-permute-done.3 = bf16[2,8320]{1,0:T(2,128)(2,1)S(1)} collective-permute-done((bf16[2,8320]{1,0:T(2,128)(2,1)S(1)}, bf16[2,8320]{1,0:T(2,128)(2,1)S(1)}, u32[]{:S(2)}, u32[]{:S(2)}) %collective-permute-start.3) | collective-permute-done | bytes 33312 | tf_op jit(solution)/shard_map/ppermute | solution.py:89
  29.4 3.2 %concatenate.16 = bf16[32,8320]{1,0:T(8,128)(2,1)S(1)} concatenate(bf16[2,8320]{1,0:T(2,128)(2,1)S(1)} %collective-permute-done.3, bf16[2,8320]{1,0:T(2,128)(2,1)S(1)} %collective-permute-done.2, bf16[2,8320]{1,0:T(2,128)(2,1)S(1)} %collective-permute-done.1, bf16[2,8320]{1,0:T(2,128)(2,1)S(1)} %collective-permute-done, bf16[2,8320]{1,0:T(2,128)(2,1)S(1)} %pad_maximum_fusion, ...), dimensions={0} | concatenate | bytes 1064960 | tf_op jit(solution)/shard_map/jit(_roll_dynamic)/concatenate | solution.py:93
  32.9 0.6 gather_fusion
  33.5 0.4 copy-done.3
  33.9 0.6 gather_fusion.1
  34.9 0.5 fusion.22
  35.5 0.5 convert_reduce_fusion.1
  35.9 0.3 fusion.10
  36.6 0.9 %copy-done.2 = bf16[1024,4,128]{2,1,0:T(4,128)(2,1)S(1)} copy-done((bf16[1024,4,128]{2,1,0:T(4,128)(2,1)S(1)}, bf16[1024,4,128]{2,1,0:T(4,128)(2,1)}, u32[]{:S(2)}) %copy-start.2) | copy-done | bytes 1048600
  37.5 0.3 fusion.4
  38.0 0.3 copy.161
  38.3 1.2 %copy.96 = f32[32,33,128]{2,1,0:T(8,128)} copy(f32[32,33,128]{2,0,1:T(8,128)S(1)} %bitcast.57) | data formatting | bytes 1081344 | tf_op jit(solution)/shard_map/reshape | solution.py:129
  39.5 2.7 %all-to-all-start = ((f32[32,33,128]{2,1,0:T(8,128)}), f32[32,33,128]{2,1,0:T(8,128)S(1)}, u32[]{:S(2)}, u32[]{:S(2)}) async-start(f32[32,33,128]{2,1,0:T(8,128)} %copy.96), calls=%async_computation | async-start | bytes 1310720 | tf_op jit(solution)/shard_map/all_to_all | solution.py:130
  42.2 0.3 select_reduce_fusion.1
  43.1 18.3 %all-to-all-done = f32[32,33,128]{2,1,0:T(8,128)S(1)} async-done(((f32[32,33,128]{2,1,0:T(8,128)}), f32[32,33,128]{2,1,0:T(8,128)S(1)}, u32[]{:S(2)}, u32[]{:S(2)}) %all-to-all-start) | async-done | bytes 540704 | tf_op jit(solution)/shard_map/all_to_all | solution.py:130
  62.0 5.2 %all_gather.3 = bf16[128,128]{1,0:T(8,128)(2,1)S(1)} all-gather(bf16[32,128]{1,0:T(8,128)(2,1)S(1)} %divide_convert_fusion), channel_id=1, replica_groups=mesh['ctx'=4,'row'=8] {'ctx'}, dimensions={0}, use_global_device_ids=true | all-gather | bytes 40960 | tf_op jit(solution)/shard_map/all_gather | solution.py:146
  67.2 0.6 reshape.144
  (67 shorter events, 3.6 us)
Async XLA Ops:
  0.0 32.9 %copy-start = (bf16[8,32,512]{2,1,0:T(8,128)(2,1)S(1)}, bf16[8,32,512]{2,1,0:T(8,128)(2,1)}, u32[]{:S(2)}) copy-start(bf16[8,32,512]{2,1,0:T(8,128)(2,1)} %param.15) | copy-start | bytes 786436
  1.6 7.9 %collective-permute-start = (bf16[2,8320]{1,0:T(2,128)(2,1)S(1)}, bf16[2,8320]{1,0:T(2,128)(2,1)S(1)}, u32[]{:S(2)}, u32[]{:S(2)}) collective-permute-start(bf16[2,8320]{1,0:T(2,128)(2,1)S(1)} %pad_maximum_fusion), channel_id=1, source_target_pairs={{0,1},{1,2},{2,3},{3,4},{4,5},{5,6},{6,7},{7,0},{8,9},{9,10},{10,1... | collective-permute-start | bytes 99848 | tf_op jit(solution)/shard_map/ppermute | solution.py:89
  4.6 6.6 %collective-permute-start.4 = (bf16[2,8320]{1,0:T(2,128)(2,1)S(1)}, bf16[2,8320]{1,0:T(2,128)(2,1)S(1)}, u32[]{:S(2)}, u32[]{:S(2)}) collective-permute-start(bf16[2,8320]{1,0:T(2,128)(2,1)S(1)} %pad_maximum_fusion), channel_id=1, source_target_pairs={{0,7},{1,0},{2,1},{3,2},{4,3},{5,4},{6,5},{7,6},{8,15},{9,8},{10,9... | collective-permute-start | bytes 99848 | tf_op jit(solution)/shard_map/ppermute | solution.py:91
  7.7 0.7 %copy-start.6 = (s32[2,32]{1,0:T(2,128)S(1)}, s32[2,32]{1,0:T(2,128)}, u32[]{:S(2)}) copy-start(s32[2,32]{1,0:T(2,128)} %param.18) | copy-start | bytes 772
  9.0 0.8 %copy-start.4 = (bf16[2,2,4096]{2,1,0:T(2,128)(2,1)S(1)}, bf16[2,2,4096]{2,1,0:T(2,128)(2,1)}, u32[]{:S(2)}) copy-start(bf16[2,2,4096]{2,1,0:T(2,128)(2,1)} %param.12) | copy-start | bytes 98308
  9.1 0.7 copy-start.7
  9.5 6.6 %collective-permute-start.1 = (bf16[2,8320]{1,0:T(2,128)(2,1)S(1)}, bf16[2,8320]{1,0:T(2,128)(2,1)S(1)}, u32[]{:S(2)}, u32[]{:S(2)}) collective-permute-start(bf16[2,8320]{1,0:T(2,128)(2,1)S(1)} %collective-permute-done), channel_id=1, source_target_pairs={{0,1},{1,2},{2,3},{3,4},{4,5},{5,6},{6,7},{7,0},{8,9},{9,10},{10,1... | collective-permute-start | bytes 99848 | tf_op jit(solution)/shard_map/ppermute | solution.py:89
  11.2 6.2 %collective-permute-start.5 = (bf16[2,8320]{1,0:T(2,128)(2,1)S(1)}, bf16[2,8320]{1,0:T(2,128)(2,1)S(1)}, u32[]{:S(2)}, u32[]{:S(2)}) collective-permute-start(bf16[2,8320]{1,0:T(2,128)(2,1)S(1)} %collective-permute-done.4), channel_id=1, source_target_pairs={{0,7},{1,0},{2,1},{3,2},{4,3},{5,4},{6,5},{7,6},{8,15},{9,8},{10,9... | collective-permute-start | bytes 99848 | tf_op jit(solution)/shard_map/ppermute | solution.py:91
  16.2 6.6 %collective-permute-start.2 = (bf16[2,8320]{1,0:T(2,128)(2,1)S(1)}, bf16[2,8320]{1,0:T(2,128)(2,1)S(1)}, u32[]{:S(2)}, u32[]{:S(2)}) collective-permute-start(bf16[2,8320]{1,0:T(2,128)(2,1)S(1)} %collective-permute-done.1), channel_id=1, source_target_pairs={{0,1},{1,2},{2,3},{3,4},{4,5},{5,6},{6,7},{7,0},{8,9},{9,10},{10,1... | collective-permute-start | bytes 99848 | tf_op jit(solution)/shard_map/ppermute | solution.py:89
  16.2 6.9 %copy-start.1 = (bf16[16,64,512]{2,1,0:T(8,128)(2,1)S(1)}, bf16[16,64,512]{2,1,0:T(8,128)(2,1)}, u32[]{:S(2)}) copy-start(bf16[16,64,512]{2,1,0:T(8,128)(2,1)} %param.17) | copy-start | bytes 3145732
  17.4 6.8 %collective-permute-start.6 = (bf16[2,8320]{1,0:T(2,128)(2,1)S(1)}, bf16[2,8320]{1,0:T(2,128)(2,1)S(1)}, u32[]{:S(2)}, u32[]{:S(2)}) collective-permute-start(bf16[2,8320]{1,0:T(2,128)(2,1)S(1)} %collective-permute-done.5), channel_id=1, source_target_pairs={{0,7},{1,0},{2,1},{3,2},{4,3},{5,4},{6,5},{7,6},{8,15},{9,8},{10,9... | collective-permute-start | bytes 99848 | tf_op jit(solution)/shard_map/ppermute | solution.py:91
  22.8 6.6 %collective-permute-start.3 = (bf16[2,8320]{1,0:T(2,128)(2,1)S(1)}, bf16[2,8320]{1,0:T(2,128)(2,1)S(1)}, u32[]{:S(2)}, u32[]{:S(2)}) collective-permute-start(bf16[2,8320]{1,0:T(2,128)(2,1)S(1)} %collective-permute-done.2), channel_id=1, source_target_pairs={{0,1},{1,2},{2,3},{3,4},{4,5},{5,6},{6,7},{7,0},{8,9},{9,10},{10,1... | collective-permute-start | bytes 99848 | tf_op jit(solution)/shard_map/ppermute | solution.py:89
  32.9 1.0 %copy-start.3 = (bf16[8,32,512]{2,1,0:T(8,128)(2,1)S(1)}, bf16[8,32,512]{2,1,0:T(8,128)(2,1)}, u32[]{:S(2)}) copy-start(bf16[8,32,512]{2,1,0:T(8,128)(2,1)} %param.14) | copy-start | bytes 786436
  36.3 1.2 %copy-start.2 = (bf16[1024,4,128]{2,1,0:T(4,128)(2,1)S(1)}, bf16[1024,4,128]{2,1,0:T(4,128)(2,1)}, u32[]{:S(2)}) copy-start(bf16[1024,4,128]{2,1,0:T(4,128)(2,1)} %reshape.132) | copy-start | bytes 3145732
  39.5 2.8 %copy-start.8 = (bf16[2,2,512]{2,1,0:T(2,128)(2,1)S(1)}, bf16[2,2,512]{2,1,0:T(2,128)(2,1)}, u32[]{:S(2)}) copy-start(bf16[2,2,512]{2,1,0:T(2,128)(2,1)} %param.20) | copy-start | bytes 12292
  39.5 3.3 %copy-start.5 = (bf16[2,2,512]{2,1,0:T(2,128)(2,1)S(1)}, bf16[2,2,512]{2,1,0:T(2,128)(2,1)}, u32[]{:S(2)}) copy-start(bf16[2,2,512]{2,1,0:T(2,128)(2,1)} %param.21) | copy-start | bytes 12292
  39.5 21.9 %all-to-all-start = ((f32[32,33,128]{2,1,0:T(8,128)}), f32[32,33,128]{2,1,0:T(8,128)S(1)}, u32[]{:S(2)}, u32[]{:S(2)}) async-start(f32[32,33,128]{2,1,0:T(8,128)} %copy.96), calls=%async_computation | async-start | bytes 1310720 | tf_op jit(solution)/shard_map/all_to_all | solution.py:130
